TPU v7x, 256 devices: a whole 4x4x8 slice. The times are simulated.
256 devices in a mesh: dp: 8 (over z), seq: 32 (over x, y, core).
Axes of the slice: x: 4, y: 4, z: 8, core: 2. Of those that a mesh axis runs over, the one named last changes fastest.
Arguments:
- inputs: bfloat16 [8, 8192, 5120], P('dp', 'seq'), may hold values from -6 to 6
- gate_proj: bfloat16 [8, 8192, 5120], P('dp', 'seq'), may hold values from -6 to 6
- write_proj: bfloat16 [8, 8192, 128], P('dp', 'seq'), may hold values from -6 to 6
- read_proj: bfloat16 [8, 8192, 128], P('dp', 'seq'), may hold values from -6 to 6
- step_size: float32 [8, 80, 8192], P('dp', None, 'seq'), may hold values from 0 to 0.4, as said below
- log_forget: float32 [8, 80, 8192], P('dp', None, 'seq'), may hold values from -0.8 to 0, as said below
- conv_weight: float32 [4, 5376], replicated, may hold values from -3 to 3
- conv_bias: float32 [5376], replicated, may hold values from -3 to 3
- skip_gain: float32 [80], replicated, may hold values from 0.5 to 1.5
- norm_gain: float32 [5120], replicated, may hold values from 0.1 to 1.9
- code_weight: bfloat16 [5120, 256], P('dp'), may hold values from -0.5 to 0.5
- prior_draw: float32 [2048, 256], P(('dp', 'seq')), may hold values from -6 to 6
Outputs:
- mixed: bfloat16 [8, 8192, 5120], P('dp', 'seq')
- codes: float32 [2048, 256], P(('dp', 'seq'))
- kernel: float32 [2048, 4096], P(('dp', 'seq'))
Inputs may be any that keep to these rules, and one draw needn't show every extreme that they name: `step_size`: positive step sizes, per document, head and position. `log_forget`: never positive.
All inputs are finite; a program needn't handle non-finite values.
Results may differ from a plain program's by a relative error of at most 0.008.
Values may be sent and summed in bfloat16 or wider, within the bound.
No kernel may reach another device: no remote copies, remote signals or barrier semaphores. Data moves between devices by JAX's collectives and lax.ppermute only.
A program may use at most 256 MiB of HBM per device.

v0:
```python
import jax
import jax.numpy as jnp
from jax import lax
from jax.sharding import PartitionSpec as P

SPAN = 128
SEG = 32


def passed_along(block, axis, distance):
    devices = range(lax.axis_size(axis))
    route = [(i - distance, i) for i in devices if i - distance in devices]
    return lax.ppermute(block, axis, route)


def carried_in(part, axis, combine, identity):
    place = lax.axis_index(axis)
    gathered = jax.tree.map(lambda a: lax.all_gather(a, axis), part)
    state = jax.tree.map(lambda a, e: jnp.zeros_like(a) + jnp.asarray(e, a.dtype), part, identity)

    def one(step, state):
        return combine(
            state, jax.tree.map(lambda a: lax.dynamic_index_in_dim(a, step, 0, False), gathered)
        )

    return lax.fori_loop(0, place, one, state)


def block_terms(values, write_rows, read_rows, steps, logs):
    cum_log = jnp.cumsum(logs, axis=1)
    length = logs.shape[1]
    causal = jnp.arange(length)[:, None] >= jnp.arange(length)[None, :]
    scores = jnp.dot(read_rows, write_rows.T, preferred_element_type=jnp.float32)
    decay = jnp.exp(jnp.where(causal[None], cum_log[:, :, None] - cum_log[:, None, :], -jnp.inf))
    mixing = (scores[None] * decay * steps[:, None, :]).astype(jnp.bfloat16)
    inner_out = jnp.einsum("hts,shp->thp", mixing, values, preferred_element_type=jnp.float32)
    tail_decay = jnp.exp(cum_log[:, -1:] - cum_log) * steps
    weighted = (tail_decay[:, :, None] * write_rows.astype(jnp.float32)[None]).astype(jnp.bfloat16)
    states = jnp.einsum("hsn,shp->hpn", weighted, values, preferred_element_type=jnp.float32)
    return (inner_out, states, cum_log)


def join_states(first, second):
    return (first[0] + second[0], jnp.exp(second[0])[:, None, None] * first[1] + second[1])


def per_device(
    inputs,
    gate_proj,
    write_proj,
    read_proj,
    step_size,
    log_forget,
    conv_weight,
    conv_bias,
    skip_gain,
    norm_gain,
    code_weight,
    prior_draw,
):
    length = inputs.shape[1]
    width = inputs.shape[2]
    state_dim = write_proj.shape[2]
    heads = step_size.shape[1]
    head_dim = width // heads
    taps = conv_weight.shape[0]
    joined = jnp.concatenate([inputs[0], write_proj[0], read_proj[0]], axis=1)
    rim_rows = passed_along(joined[length - (taps - 1) :], "seq", 1)
    padded = jnp.concatenate([rim_rows, joined], axis=0)
    summed = conv_bias[None, :] + conv_weight[0][None, :] * padded[0:length].astype(jnp.float32)
    for offset in range(1, taps):
        summed = summed + conv_weight[offset][None, :] * padded[offset : offset + length].astype(
            jnp.float32
        )
    active = jax.nn.silu(summed).astype(jnp.bfloat16)
    values = active[:, :width].reshape(length, heads, head_dim)
    write_all = active[:, width : width + state_dim]
    read_all = active[:, width + state_dim :]
    steps = step_size[0]
    logs = log_forget[0]
    blocks = length // SPAN
    inner_list = []
    state_list = []
    cum_list = []
    for block in range(blocks):
        lower = block * SPAN
        upper = lower + SPAN
        inner_out, states, cum_log = block_terms(
            values[lower:upper],
            write_all[lower:upper],
            read_all[lower:upper],
            steps[:, lower:upper],
            logs[:, lower:upper],
        )
        inner_list.append(inner_out)
        state_list.append(states)
        cum_list.append(cum_log)
    running = jnp.zeros((heads, head_dim, state_dim), jnp.float32)
    before = jnp.zeros((heads,), jnp.float32)
    start_list = []
    before_list = []
    for block in range(blocks):
        start_list.append(running)
        before_list.append(before)
        block_total = cum_list[block][:, -1]
        running = jnp.exp(block_total)[:, None, None] * running + state_list[block]
        before = before + block_total
    identity = (jnp.zeros_like(before), jnp.zeros_like(running))
    decay_in, carry_in = carried_in((before, running), "seq", join_states, identity)
    outputs = []
    for block in range(blocks):
        lower = block * SPAN
        upper = lower + SPAN
        start = start_list[block] + jnp.exp(before_list[block])[:, None, None] * carry_in
        read_block = read_all[lower:upper].astype(jnp.float32)
        outer_out = jnp.exp(cum_list[block]).T[:, :, None] * jnp.einsum(
            "tn,hpn->thp", read_block, start, precision=lax.Precision.HIGHEST
        )
        outputs.append(inner_list[block] + outer_out)
    ssd_out = jnp.concatenate(outputs, axis=0)
    total = ssd_out + skip_gain[None, :, None] * values.astype(jnp.float32)
    gated = total.reshape(length, width) * jax.nn.silu(gate_proj[0].astype(jnp.float32))
    scale = lax.rsqrt(jnp.mean(gated * gated, axis=1, keepdims=True) + 1e-05)
    mixed = (gated * scale * norm_gain[None, :]).astype(jnp.bfloat16)
    pooled = jnp.mean(mixed.astype(jnp.float32).reshape(length // SEG, SEG, width), axis=1).astype(
        jnp.bfloat16
    )
    codes_local = jnp.dot(
        pooled,
        lax.all_gather(code_weight, "dp", axis=0, tiled=True),
        preferred_element_type=jnp.float32,
    )
    all_codes, all_prior = (
        lax.all_gather(codes_local, ("dp", "seq"), axis=0, tiled=True),
        lax.all_gather(prior_draw, ("dp", "seq"), axis=0, tiled=True),
    )
    columns = jnp.concatenate([all_codes, all_prior], axis=0)
    cross = jnp.dot(codes_local, columns.T, precision=lax.Precision.HIGHEST)
    row_sq = jnp.sum(codes_local * codes_local, axis=1)
    col_sq = jnp.sum(columns * columns, axis=1)
    dist_sq = row_sq[:, None] + col_sq[None, :] - 2.0 * cross
    code_dim = codes_local.shape[1]
    kernel = 2.0 * code_dim / (2.0 * code_dim + dist_sq)
    return (mixed[None], codes_local, kernel)


def solution(mesh):
    in_specs = (
        P("dp", "seq", None),
        P("dp", "seq", None),
        P("dp", "seq", None),
        P("dp", "seq", None),
        P("dp", None, "seq"),
        P("dp", None, "seq"),
        P(),
        P(),
        P(),
        P(),
        P("dp", None),
        P(("dp", "seq"), None),
    )
    out_specs = (P("dp", "seq", None), P(("dp", "seq"), None), P(("dp", "seq"), None))
    return jax.shard_map(
        per_device, mesh=mesh, in_specs=in_specs, out_specs=out_specs, check_vma=False
    )
```

profile of v0, /device:TPU:1, one launch (start us, length us, event | category | flops | bytes accessed | tf_op | source)
XLA Modules:
  0.0 618.8 jit_solution(9493338200007290373)
XLA Ops:
  7.3 2.1 pad_maximum_fusion
  9.5 4.6 collective-permute-start
  15.3 2.4 maximum_maximum_fusion
  17.7 4.4 multiply_convert_fusion
  22.2 2.0 fusion.52
  24.2 2.4 copy.31
  26.6 2.4 copy.32
  29.0 3.9 fusion.9
  33.0 1.5 copy-done.6
  34.4 4.0 multiply_add_fusion
  40.9 126.3 %all-reduce = f32[2560]{0:T(1024)S(1)} all-reduce(f32[2560]{0:T(1024)S(1)} %dynamic-update-slice), channel_id=2, replica_groups=mesh['dp'=8,'seq'=32] {'seq'}, use_global_device_ids=true, to_apply=%add | all-reduce | flops 2560 | bytes 20480
  167.5 4.5 fusion.7
  172.2 4.1 fusion.8
  176.2 116.8 %all-gather.13.cloned.1.call-done = f32[2560,64,128]{2,1,0:T(8,128)} async-done(((f32[80,64,128]{2,1,0:T(8,128)}), f32[2560,64,128]{2,1,0:T(8,128)}) %all-gather.13.cloned.1.call-update) | async-done | bytes 83886096 | tf_op jit(solution)/shard_map/all_gather | solution.py:18
  293.4 2.4 while.12
  293.4 2.2 bitcast_add_fusion.4
  295.8 4.6 bitcast_add_fusion.2
  300.4 3.2 copy.37
  303.6 5.7 bitcast_add_fusion.1
  309.3 3.4 copy.38
  312.7 5.3 multiply_reduce_fusion
  318.1 2.3 copy-done
  320.3 1.0 convert_reduce_fusion
  321.3 11.0 %all-gather.7.cloned.1.call-done = bf16[5120,256]{1,0:T(8,128)(2,1)} async-done(((bf16[640,256]{1,0:T(8,128)(2,1)}), bf16[5120,256]{1,0:T(8,128)(2,1)}) %all-gather.7.cloned.1.call-update) | async-done | bytes 2621456 | tf_op jit(solution)/shard_map/all_gather | solution.py:130
  332.3 2.9 multiply_reduce_fusion.2
  335.8 4.7 fusion.50
  340.5 154.3 %all-gather.9.cloned.1.call-done = f32[2048,256]{1,0:T(8,128)} async-done(((f32[8,256]{1,0:T(8,128)}), f32[2048,256]{1,0:T(8,128)}) %all-gather.9.cloned.1.call-update) | async-done | bytes 2097168 | tf_op jit(solution)/shard_map/all_gather | solution.py:134
  494.8 3.1 constant_dynamic-update-slice_fusion.1
  497.9 103.6 %all-gather.11.cloned.1.call-done = f32[2048,256]{1,0:T(8,128)} async-done(((f32[8,256]{1,0:T(8,128)}), f32[2048,256]{1,0:T(8,128)}) %all-gather.11.cloned.1.call-update) | async-done | bytes 2097168 | tf_op jit(solution)/shard_map/all_gather | solution.py:135
  601.5 3.0 constant_dynamic-update-slice_fusion
  604.6 3.0 multiply_reduce_fusion.1
  608.0 4.2 fusion.6
  (67 shorter events, 4.9 us)
Async XLA Ops:
  7.2 285.9 %all-gather.13.cloned.1.call-start = ((), (), s32[]{:S(2)}) async-start(), calls=%async_computation.3 | async-start | bytes 86507520 | tf_op jit(solution)/shard_map/all_gather | solution.py:18
  7.2 6.8 %copy-start.13 = (f32[1,80,256]{2,1,0:T(8,128)S(1)}, f32[1,80,256]{2,1,0:T(8,128)}, u32[]{:S(2)}) copy-start(f32[1,80,256]{2,1,0:T(8,128)} %param.19) | copy-start | bytes 245764
  7.2 7.7 %copy-start.14 = (f32[1,80,256]{2,1,0:T(8,128)S(1)}, f32[1,80,256]{2,1,0:T(8,128)}, u32[]{:S(2)}) copy-start(f32[1,80,256]{2,1,0:T(8,128)} %param.18) | copy-start | bytes 245764
  7.2 7.8 %copy-start.11 = (f32[4,5376]{1,0:T(4,128)S(1)}, f32[4,5376]{1,0:T(4,128)}, u32[]{:S(2)}) copy-start(f32[4,5376]{1,0:T(4,128)} %param.20) | copy-start | bytes 258052
  7.2 8.1 %copy-start.4 = (bf16[1,256,5120]{2,1,0:T(8,128)(2,1)S(1)}, bf16[1,256,5120]{2,1,0:T(8,128)(2,1)}, u32[]{:S(2)}) copy-start(bf16[1,256,5120]{2,1,0:T(8,128)(2,1)} %param.14) | copy-start | bytes 7864324
  7.3 8.1 %copy-start.9 = (bf16[1,256,128]{2,1,0:T(8,128)(2,1)S(1)}, bf16[1,256,128]{2,1,0:T(8,128)(2,1)}, u32[]{:S(2)}) copy-start(bf16[1,256,128]{2,1,0:T(8,128)(2,1)} %param.17) | copy-start | bytes 196612
  7.3 8.1 %copy-start.10 = (bf16[1,256,128]{2,1,0:T(8,128)(2,1)S(1)}, bf16[1,256,128]{2,1,0:T(8,128)(2,1)}, u32[]{:S(2)}) copy-start(bf16[1,256,128]{2,1,0:T(8,128)(2,1)} %param.16) | copy-start | bytes 196612
  9.5 5.8 collective-permute-start
  15.3 2.4 copy-start.5
  15.3 2.4 copy-start.16
  22.2 149.9 %copy-start.2 = (bf16[256,5376]{1,0:T(8,128)(2,1)}, bf16[256,5376]{1,0:T(8,128)(2,1)S(1)}, u32[]{:S(2)}) copy-start(bf16[256,5376]{1,0:T(8,128)(2,1)S(1)} %multiply_convert_fusion) | copy-start | bytes 8257540
  29.0 5.4 copy-start.7
  33.0 1.5 copy-start.6
  38.5 0.9 copy-start.18
  38.5 128.8 %copy-start.17 = (f32[80]{0:T(128)S(1)}, f32[80]{0:T(128)}, u32[]{:S(2)}) copy-start(f32[80]{0:T(128)} %param.22) | copy-start | bytes 964
  38.5 293.8 %all-gather.7.cloned.1.call-start = ((), (), s32[]{:S(2)}) async-start(), calls=%async_computation | async-start | bytes 2949120 | tf_op jit(solution)/shard_map/all_gather | solution.py:130
  39.3 455.6 %all-gather.9.cloned.1.call-start = ((), (), s32[]{:S(2)}) async-start(), calls=%async_computation.1 | async-start | bytes 2105344 | tf_op jit(solution)/shard_map/all_gather | solution.py:134
  167.5 4.7 copy-start.8
  309.3 3.4 copy-start.3
  312.7 7.6 %copy-start.12 = (f32[5120]{0:T(1024)S(1)}, f32[5120]{0:T(1024)}, u32[]{:S(2)}) copy-start(f32[5120]{0:T(1024)} %param.23) | copy-start | bytes 61444
  318.0 2.3 copy-start
  335.3 266.3 %all-gather.11.cloned.1.call-start = ((), (), s32[]{:S(2)}) async-start(), calls=%async_computation.2 | async-start | bytes 2105344 | tf_op jit(solution)/shard_map/all_gather | solution.py:135
  604.6 3.4 copy-start.1
  604.6 3.4 copy-start.15
Sparse Core Ops, SparseCore 0:
  38.6 254.3 all-gather.12
  294.8 37.4 all-gather.6
  336.6 158.1 all-gather.8
  498.4 103.0 all-gather.10
where the time goes:
time: 620 us; the launch traced here: 619 us
  waiting for transfers between devices  387 us (62%)
  blocking collectives  126 us (20%)
  matrix products  34.3 us (6%)
  other arithmetic  26 us (4%)
  local copies, waits for them, and re-layouts  25.5 us (4%)
  between operations  14.8 us (2%)
    all_gather x1, waiting for transfers between devices, per_device(): lax.all_gather(codes_local, ('dp', 'seq'), axis=0, tiled=True)  154 us
    unnamed x1, blocking collectives  126 us
    all_gather x1, waiting for transfers between devices, carried_in(): gathered = jax.tree.map(lambda a: lax.all_gather(a, axis), part)  117 us
    all_gather x1, waiting for transfers between devices, per_device(): lax.all_gather(prior_draw, ('dp', 'seq'), axis=0, tiled=True)  104 us
  transfers between devices with their start and end apart: 5, of which 4 were waited for; matrix products, arithmetic and copies ran while one was open for 7% of the time, Pallas kernels for 0%

commit v1 on v0

--- a/solution.py
+++ b/solution.py
@@ -131,7 +131,12 @@
         preferred_element_type=jnp.float32,
     )
     all_codes, all_prior = (
-        lax.all_gather(codes_local, ("dp", "seq"), axis=0, tiled=True),
+        jnp.concatenate(
+            lax.all_to_all(
+                jnp.stack([codes_local] * lax.axis_size(("dp", "seq"))), ("dp", "seq"), 0, 0
+            ),
+            axis=0,
+        ),
         lax.all_gather(prior_draw, ("dp", "seq"), axis=0, tiled=True),
     )
     columns = jnp.concatenate([all_codes, all_prior], axis=0)

time: 620 us -> 474 us (0.76)
  waiting for transfers between devices: 387 us -> 180 us
  starting transfers between devices: 4.74 us -> 71.5 us
    all_gather x1 -> x0, waiting for transfers between devices: 154 us -> none  [per_device(): lax.all_gather(codes_local, ('dp', 'seq'), axis=0, tiled=True)]
    all_to_all x0 -> x1, starting transfers between devices: none -> 66.8 us  [per_device(): lax.all_to_all(jnp.stack([codes_local] * lax.axis_size(('dp', 'seq'))), (...]
    all_gather x1, waiting for transfers between devices: 104 us -> 45 us  [per_device(): lax.all_gather(prior_draw, ('dp', 'seq'), axis=0, tiled=True)]
    all_to_all x0 -> x1, waiting for transfers between devices: none -> 6.76 us  [per_device(): lax.all_to_all(jnp.stack([codes_local] * lax.axis_size(('dp', 'seq'))), (...]
  transfers between devices with their start and end apart: 5 -> 5, of which waited for: 4 -> 4; matrix products, arithmetic and copies ran while one was open for 7% -> 10% of each run, Pallas kernels for 0% -> 0%
where the time goes in v1:
time: 474 us; the launch traced here: 473 us
  waiting for transfers between devices  180 us (38%)
  blocking collectives  126 us (27%)
  starting transfers between devices  71.5 us (15%)
  matrix products  33.7 us (7%)
  other arithmetic  25.4 us (5%)
  local copies, waits for them, and re-layouts  20.5 us (4%)
  between operations  14.8 us (3%)
    unnamed x1, blocking collectives  126 us
    all_gather x1, waiting for transfers between devices, carried_in(): gathered = jax.tree.map(lambda a: lax.all_gather(a, axis), part)  116 us
    all_to_all x1, starting transfers between devices, per_device(): lax.all_to_all(jnp.stack([codes_local] * lax.axis_size(('dp', 'seq'))), (...  66.8 us
    all_gather x1, waiting for transfers between devices, per_device(): lax.all_gather(prior_draw, ('dp', 'seq'), axis=0, tiled=True)  45 us
    all_gather x1, waiting for transfers between devices, per_device(): lax.all_gather(code_weight, 'dp', axis=0, tiled=True)  10.9 us
    dot_general x2, matrix products, per_device(): jnp.einsum('tn,hpn->thp', read_block, start, precision=lax.Precision.HIGH...  10.4 us
  transfers between devices with their start and end apart: 5, of which 4 were waited for; matrix products, arithmetic and copies ran while one was open for 10% of the time, Pallas kernels for 0%

profile of v1, /device:TPU:1, one launch (start us, length us, event | category | flops | bytes accessed | tf_op | source)
XLA Modules:
  0.0 472.6 jit_solution(2061476366741321254)
XLA Ops:
  7.3 2.1 pad_maximum_fusion.2
  9.5 4.6 collective-permute-start
  15.3 2.4 maximum_maximum_fusion
  17.7 4.4 multiply_convert_fusion
  22.2 2.0 fusion.53
  24.2 2.4 copy.31
  26.6 2.4 copy.32
  29.0 3.9 fusion.9
  33.0 1.5 copy-done.5
  34.4 4.0 multiply_add_fusion
  41.6 126.4 %all-reduce = f32[2560]{0:T(1024)S(1)} all-reduce(f32[2560]{0:T(1024)S(1)} %dynamic-update-slice), channel_id=2, replica_groups=mesh['dp'=8,'seq'=32] {'seq'}, use_global_device_ids=true, to_apply=%add | all-reduce | flops 2560 | bytes 20480
  168.5 4.5 fusion.7
  173.0 4.0 fusion.8
  177.1 116.0 %all-gather.10.cloned.1.call-done = f32[2560,64,128]{2,1,0:T(8,128)} async-done(((f32[80,64,128]{2,1,0:T(8,128)}), f32[2560,64,128]{2,1,0:T(8,128)}) %all-gather.10.cloned.1.call-update) | async-done | bytes 83886096 | tf_op jit(solution)/shard_map/all_gather | solution.py:18
  293.4 2.4 while.12
  293.4 2.2 bitcast_add_fusion.4
  295.8 4.6 bitcast_add_fusion.2
  300.4 3.2 copy.37
  303.7 5.7 %bitcast_add_fusion.1 = f32[128,80,64]{0,2,1:T(8,128)} fusion(f32[80,64,128]{2,1,0:T(8,128)} %fusion.8, f32[80,64,128]{2,1,0:T(8,128)S(1)} %get-tuple-element.47, f32[80,64,128]{2,1,0:T(8,128)} %copy-done.5, f32[80]{0:T(128)S(1)} %get-tuple-element.79, f32[128,80]{0,1:T(8,128)S(1)} %get-tuple-element.77, f32[80]{0:T(128)S(1)} %get-tuple-element.80, ...), kind=kOutput, calls=%fused_computation.29 | convolution fusion | flops 1009909760 | bytes 10560128 | tf_op jit(solution)/shard_map/tn,hpn->thp/dot_general | solution.py:116
  309.4 3.4 copy.38
  312.8 5.3 %multiply_reduce_fusion = (f32[256]{0:T(256)S(1)}, f32[256,5120]{1,0:T(8,128)S(1)}) fusion(bf16[1,256,5120]{2,1,0:T(8,128)(2,1)} %param.15, bf16[256,5376]{1,0:T(8,128)(2,1)S(1)} %copy-done.2, f32[5120]{0:T(1024)S(1)} %mul.252, f32[128,5120]{1,0:T(8,128)} %copy.38, f32[128,5120]{1,0:T(8,128)} %copy.37), kind=kLoop, calls=%fused_computation.12 | loop fusion | flops 15728384 | bytes 15750144 | tf_op jit(solution)/shard_map/reduce_sum | solution.py:123
  318.1 2.3 copy-done
  320.4 1.0 convert_reduce_fusion
  321.4 10.9 %all-gather.6.cloned.1.call-done = bf16[5120,256]{1,0:T(8,128)(2,1)} async-done(((bf16[640,256]{1,0:T(8,128)(2,1)}), bf16[5120,256]{1,0:T(8,128)(2,1)}) %all-gather.6.cloned.1.call-update) | async-done | bytes 2621456 | tf_op jit(solution)/shard_map/all_gather | solution.py:130
  332.4 2.3 multiply_reduce_fusion.2
  334.7 1.5 stack.2
  336.2 66.8 %all-to-all-start = ((f32[256,8,256]{2,1,0:T(8,128)}), f32[256,8,256]{2,1,0:T(8,128)S(1)}, u32[]{:S(2)}, u32[]{:S(2)}) async-start(f32[256,8,256]{2,1,0:T(8,128)} %stack.2), calls=%async_computation | async-start | bytes 4194304 | tf_op jit(solution)/shard_map/all_to_all | solution.py:135
  403.0 4.7 fusion.51
  407.7 45.0 %all-gather.8.cloned.1.call-done = f32[2048,256]{1,0:T(8,128)} async-done(((f32[8,256]{1,0:T(8,128)}), f32[2048,256]{1,0:T(8,128)}) %all-gather.8.cloned.1.call-update) | async-done | bytes 2097168 | tf_op jit(solution)/shard_map/all_gather | solution.py:140
  452.7 6.8 %all-to-all-done = f32[256,8,256]{2,1,0:T(8,128)S(1)} async-done(((f32[256,8,256]{2,1,0:T(8,128)}), f32[256,8,256]{2,1,0:T(8,128)S(1)}, u32[]{:S(2)}, u32[]{:S(2)}) %all-to-all-start) | async-done | bytes 2097184 | tf_op jit(solution)/shard_map/all_to_all | solution.py:135
  459.5 2.4 multiply_reduce_fusion.1
  461.9 4.2 fusion.6
  (65 shorter events, 4.5 us)
Async XLA Ops:
  7.2 285.9 %all-gather.10.cloned.1.call-start = ((), (), s32[]{:S(2)}) async-start(), calls=%async_computation.3 | async-start | bytes 86507520 | tf_op jit(solution)/shard_map/all_gather | solution.py:18
  7.2 6.8 %copy-start.13 = (f32[1,80,256]{2,1,0:T(8,128)S(1)}, f32[1,80,256]{2,1,0:T(8,128)}, u32[]{:S(2)}) copy-start(f32[1,80,256]{2,1,0:T(8,128)} %param.19) | copy-start | bytes 245764
  7.2 7.7 %copy-start.14 = (f32[1,80,256]{2,1,0:T(8,128)S(1)}, f32[1,80,256]{2,1,0:T(8,128)}, u32[]{:S(2)}) copy-start(f32[1,80,256]{2,1,0:T(8,128)} %param.18) | copy-start | bytes 245764
  7.2 7.8 %copy-start.11 = (f32[4,5376]{1,0:T(4,128)S(1)}, f32[4,5376]{1,0:T(4,128)}, u32[]{:S(2)}) copy-start(f32[4,5376]{1,0:T(4,128)} %param.20) | copy-start | bytes 258052
  7.2 8.1 %copy-start.3 = (bf16[1,256,5120]{2,1,0:T(8,128)(2,1)S(1)}, bf16[1,256,5120]{2,1,0:T(8,128)(2,1)}, u32[]{:S(2)}) copy-start(bf16[1,256,5120]{2,1,0:T(8,128)(2,1)} %param.14) | copy-start | bytes 7864324
  7.3 8.1 %copy-start.9 = (bf16[1,256,128]{2,1,0:T(8,128)(2,1)S(1)}, bf16[1,256,128]{2,1,0:T(8,128)(2,1)}, u32[]{:S(2)}) copy-start(bf16[1,256,128]{2,1,0:T(8,128)(2,1)} %param.17) | copy-start | bytes 196612
  7.3 8.1 %copy-start.10 = (bf16[1,256,128]{2,1,0:T(8,128)(2,1)S(1)}, bf16[1,256,128]{2,1,0:T(8,128)(2,1)}, u32[]{:S(2)}) copy-start(bf16[1,256,128]{2,1,0:T(8,128)(2,1)} %param.16) | copy-start | bytes 196612
  9.5 5.8 %collective-permute-start = (bf16[3,5376]{1,0:T(4,128)(2,1)S(1)}, bf16[3,5376]{1,0:T(4,128)(2,1)S(1)}, u32[]{:S(2)}, u32[]{:S(2)}) collective-permute-start(bf16[3,5376]{1,0:T(4,128)(2,1)S(1)} %slice.104), channel_id=1, source_target_pairs={{0,1},{1,2},{2,3},{3,4},{4,5},{5,6},{6,7},{7,8},{8,9},{9,10},{10,1... | collective-permute-start | bytes 96776 | tf_op jit(solution)/shard_map/ppermute | solution.py:13
  15.3 2.4 copy-start.4
  15.3 2.4 copy-start.16
  22.2 146.1 %copy-start.1 = (bf16[256,5376]{1,0:T(8,128)(2,1)}, bf16[256,5376]{1,0:T(8,128)(2,1)S(1)}, u32[]{:S(2)}) copy-start(bf16[256,5376]{1,0:T(8,128)(2,1)S(1)} %multiply_convert_fusion) | copy-start | bytes 8257540
  29.0 5.4 %copy-start.7 = (bf16[128,5120]{0,1:T(8,128)(2,1)S(1)}, bf16[128,5120]{0,1:T(8,128)(2,1)}, u32[]{:S(2)}) copy-start(bf16[128,5120]{0,1:T(8,128)(2,1)} %copy.32) | copy-start | bytes 3932164
  33.0 1.5 copy-start.5
  38.5 1.6 copy-start.18
  38.5 129.6 %copy-start.17 = (f32[80]{0:T(128)S(1)}, f32[80]{0:T(128)}, u32[]{:S(2)}) copy-start(f32[80]{0:T(128)} %param.22) | copy-start | bytes 964
  38.5 293.9 %all-gather.6.cloned.1.call-start = ((), (), s32[]{:S(2)}) async-start(), calls=%async_computation.1 | async-start | bytes 2949120 | tf_op jit(solution)/shard_map/all_gather | solution.py:130
  39.3 413.5 %all-gather.8.cloned.1.call-start = ((), (), s32[]{:S(2)}) async-start(), calls=%async_computation.2 | async-start | bytes 2105344 | tf_op jit(solution)/shard_map/all_gather | solution.py:140
  168.5 4.6 copy-start.8
  309.4 3.4 copy-start.2
  312.8 7.6 %copy-start.12 = (f32[5120]{0:T(1024)S(1)}, f32[5120]{0:T(1024)}, u32[]{:S(2)}) copy-start(f32[5120]{0:T(1024)} %param.23) | copy-start | bytes 61444
  318.1 2.3 copy-start
  334.7 127.2 %copy-start.15 = (f32[8,256]{1,0:T(8,128)}, f32[8,256]{1,0:T(8,128)S(1)}, u32[]{:S(2)}) copy-start(f32[8,256]{1,0:T(8,128)S(1)} %get-tuple-element.82) | copy-start | bytes 24580
  336.2 123.3 %all-to-all-start = ((f32[256,8,256]{2,1,0:T(8,128)}), f32[256,8,256]{2,1,0:T(8,128)S(1)}, u32[]{:S(2)}, u32[]{:S(2)}) async-start(f32[256,8,256]{2,1,0:T(8,128)} %stack.2), calls=%async_computation | async-start | bytes 4194304 | tf_op jit(solution)/shard_map/all_to_all | solution.py:135
  459.5 2.4 copy-start.6
Sparse Core Ops, SparseCore 0:
  38.6 254.3 all-gather.9
  294.8 37.4 all-gather.5
  336.1 116.6 all-gather.7
